TPU v7x, 128 devices: a whole 4x4x4 slice. The times are simulated.
128 devices in a mesh: seq: 16 (over x_lo, z, core), batch: 8 (over y, x_hi).
Axes of the slice: x: 4 (x_hi: 2, x_lo: 2; x = x_hi * 2 + x_lo), y: 4, z: 4, core: 2. Of those that a mesh axis runs over, the one named last changes fastest.
Arguments:
- activations: bfloat16 [2, 8192, 1536], P(None, ('seq', 'batch')), may hold values from -6 to 6
- conv_gain: float32 [1536], replicated, may hold values from 0.25 to 1.75
- conv_weight: bfloat16 [5, 1536, 1536], P(None, 'batch'), may hold values from -0.0625 to 0.0625
- attention_gain: float32 [1536], replicated, may hold values from 0.25 to 1.75
- query_weight: bfloat16 [1536, 1536], P('batch'), may hold values from -3 to 3
- key_weight: bfloat16 [1536, 1536], P('batch'), may hold values from -3 to 3
- value_weight: bfloat16 [1536, 1536], P('batch'), may hold values from -0.15625 to 0.15625
- output_weight: bfloat16 [1536, 1536], P('batch'), may hold values from -0.15625 to 0.15625
Outputs:
- block_out: bfloat16 [2, 8192, 1536], P(None, ('seq', 'batch'))
All inputs are finite; a program needn't handle non-finite values.
Results may differ from a plain program's by a relative error of at most 0.015.
Values may be sent and summed in bfloat16 or wider, within the bound.
No kernel may reach another device: no remote copies, remote signals or barrier semaphores. Data moves between devices by JAX's collectives and lax.ppermute only.
A program may use at most 128 MiB of HBM per device.

v0:
```python
import math
import jax
import jax.numpy as jnp
from jax import lax
from jax.sharding import PartitionSpec as P

HD = 192


def with_halo(cells, sides, width):
    for axis, dim in sides:
        count = lax.axis_size(axis)
        ends = count - 1
        head = lax.slice_in_dim(cells, 0, width, axis=dim)
        tail = lax.slice_in_dim(cells, cells.shape[dim] - width, cells.shape[dim], axis=dim)
        cells = jnp.concatenate(
            [
                lax.ppermute(tail, axis, [(i, (i + 1) % count) for i in range(ends)]),
                cells,
                lax.ppermute(head, axis, [((i + 1) % count, i) for i in range(ends)]),
            ],
            axis=dim,
        )
    return cells


def gather_batch(block, axis):
    count = lax.axis_size("batch")
    copies = jnp.broadcast_to(block[None], (count,) + block.shape)
    arrived = jnp.moveaxis(lax.all_to_all(copies, "batch", 0, 0, tiled=False), 0, axis)
    return arrived.reshape(
        block.shape[:axis] + (count * block.shape[axis],) + block.shape[axis + 1 :]
    )


def normalize(rows_in, gain):
    values = rows_in.astype(jnp.float32)
    scale = lax.rsqrt(jnp.mean(values * values, axis=-1, keepdims=True) + 1e-06)
    return values * scale * gain


def one_sample(
    activations,
    conv_gain,
    conv_weight,
    attention_gain,
    query_weight,
    key_weight,
    value_weight,
    output_weight,
):
    sample_count, own_rows, full_width = activations.shape
    tap_count, local_out, _ = conv_weight.shape
    flank_rows = tap_count // 2
    gathered_in = gather_batch(activations, 1)
    seq_rows = gathered_in.shape[1]
    active = jax.nn.gelu(normalize(gathered_in, conv_gain)).astype(jnp.bfloat16)
    framed = with_halo(active, (("seq", 1),), flank_rows)
    conv_sum = jnp.zeros((sample_count, local_out, seq_rows), jnp.float32)
    for offset in range(tap_count):
        conv_sum = conv_sum + jnp.einsum(
            "std,ed->set",
            framed[:, offset : offset + seq_rows],
            conv_weight[offset],
            preferred_element_type=jnp.float32,
        )
    column_start = lax.axis_index("batch") * local_out
    own_columns = lax.dynamic_slice_in_dim(gathered_in, column_start, local_out, 2)
    residual = jnp.transpose(own_columns, (0, 2, 1)).astype(jnp.float32)
    hidden_part = (residual + conv_sum).astype(jnp.bfloat16)
    hidden_full = gather_batch(hidden_part, 1)
    hidden_float = hidden_full.astype(jnp.float32)
    norm_scale = lax.rsqrt(jnp.mean(hidden_float * hidden_float, axis=1, keepdims=True) + 1e-06)
    normed = (hidden_float * norm_scale * attention_gain[None, :, None]).astype(jnp.bfloat16)
    queries = (
        jnp.einsum("sdt,ed->set", normed, query_weight, preferred_element_type=jnp.float32)
        * HD ** (-0.5)
    ).astype(jnp.bfloat16)
    key_rows = jnp.einsum(
        "sdt,ed->set", normed, key_weight, preferred_element_type=jnp.float32
    ).astype(jnp.bfloat16)
    value_rows = jnp.einsum(
        "sdt,ed->set", normed, value_weight, preferred_element_type=jnp.float32
    ).astype(jnp.bfloat16)
    heads_here = query_weight.shape[0] // HD
    query_heads = queries.reshape(sample_count, heads_here, HD, seq_rows)
    start_max = jnp.full((sample_count, heads_here, seq_rows), -jnp.inf, jnp.float32)
    start_sum = jnp.zeros((sample_count, heads_here, seq_rows), jnp.float32)
    start_acc = jnp.zeros((sample_count, heads_here, HD, seq_rows), jnp.float32)
    key_tile = lax.all_gather(key_rows, "seq", axis=2, tiled=True)
    value_tile = lax.all_gather(value_rows, "seq", axis=2, tiled=True)
    key_count = key_tile.shape[2]
    block_rows = math.gcd(key_count, 512)

    def consume(block_index, running):
        running_max, weight_sum, summed = running
        begin = block_index * block_rows
        key_block = lax.dynamic_slice_in_dim(key_tile, begin, block_rows, 2).reshape(
            sample_count, heads_here, HD, block_rows
        )
        value_block = lax.dynamic_slice_in_dim(value_tile, begin, block_rows, 2).reshape(
            sample_count, heads_here, HD, block_rows
        )
        scores = jnp.einsum(
            "shdq,shdk->shqk", query_heads, key_block, preferred_element_type=jnp.float32
        )
        new_max = jnp.maximum(running_max, jnp.max(scores, axis=-1))
        weights = jnp.exp(scores - new_max[..., None])
        rescale = jnp.exp(running_max - new_max)
        weight_sum = weight_sum * rescale + jnp.sum(weights, axis=-1)
        summed = summed * rescale[:, :, None, :] + jnp.einsum(
            "shqk,shdk->shdq",
            weights.astype(jnp.bfloat16),
            value_block,
            preferred_element_type=jnp.float32,
        )
        return (new_max, weight_sum, summed)

    final_max, weight_sum, summed = lax.fori_loop(
        0, key_count // block_rows, consume, (start_max, start_sum, start_acc)
    )
    attended = (
        (summed / weight_sum[:, :, None, :])
        .astype(jnp.bfloat16)
        .reshape(sample_count, heads_here * HD, seq_rows)
    )
    row_start = lax.axis_index("batch") * own_rows
    own_hidden = jnp.transpose(
        lax.dynamic_slice_in_dim(hidden_full, row_start, own_rows, 2), (0, 2, 1)
    ).astype(jnp.float32)
    batch_count = lax.axis_size("batch")
    partial_rows = jnp.einsum(
        "set,ef->tsf", attended, output_weight, preferred_element_type=jnp.float32
    ).astype(jnp.bfloat16)
    partial_rows = partial_rows.reshape(batch_count, own_rows, sample_count, full_width)
    share_rows = jnp.sum(
        lax.all_to_all(partial_rows, "batch", 0, 0, tiled=False).astype(jnp.float32), axis=0
    )
    branch_rows = jnp.transpose(share_rows, (1, 0, 2))
    result = own_hidden + branch_rows
    return result.astype(jnp.bfloat16)


def shards(activations, *weights):
    pieces = [
        one_sample(activations[sample : sample + 1], *weights)
        for sample in range(activations.shape[0])
    ]
    return jnp.concatenate(pieces, axis=0)


def solution(mesh):
    placed = (
        P(None, ("seq", "batch"), None),
        P(),
        P(None, "batch", None),
        P(),
        P("batch", None),
        P("batch", None),
        P("batch", None),
        P("batch", None),
    )
    return jax.shard_map(
        shards,
        mesh=mesh,
        in_specs=placed,
        out_specs=P(None, ("seq", "batch"), None),
        check_vma=False,
    )
```

profile of v0, /device:TPU:0, one launch (start us, length us, event | category | flops | bytes accessed | tf_op | source)
XLA Modules:
  0.0 390.3 jit_solution(14848912916177011553)
XLA Ops:
  7.8 29.6 %all_to_all.30 = bf16[8,1,64,1536]{3,2,1,0:T(8,128)(2,1)S(1)} all-to-all(bf16[8,1,64,1536]{3,2,1,0:T(8,128)(2,1)S(1)} %broadcast_in_dim.27), channel_id=1, replica_groups=mesh['seq'=16,'batch'=8] {'batch'}, dimensions={0} | all-to-all | bytes 3145728 | tf_op jit(solution)/shard_map/all_to_all | solution.py:30
  38.7 4.4 %all-to-all-start.3 = ((bf16[8,1,64,1536]{3,2,1,0:T(8,128)(2,1)}), bf16[8,1,64,1536]{3,2,1,0:T(8,128)(2,1)}, u32[]{:S(2)}, u32[]{:S(2)}) async-start(bf16[8,1,64,1536]{3,2,1,0:T(8,128)(2,1)} %broadcast_in_dim.33), calls=%async_computation.3 | async-start | bytes 3145728 | tf_op jit(solution)/shard_map/all_to_all | solution.py:30
  43.6 21.5 %all-to-all-done.3 = bf16[8,1,64,1536]{3,2,1,0:T(8,128)(2,1)} async-done(((bf16[8,1,64,1536]{3,2,1,0:T(8,128)(2,1)}), bf16[8,1,64,1536]{3,2,1,0:T(8,128)(2,1)}, u32[]{:S(2)}, u32[]{:S(2)}) %all-to-all-start.3) | async-done | bytes 1572896 | tf_op jit(solution)/shard_map/all_to_all | solution.py:30
  65.1 1.8 fusion.41
  68.3 4.0 %fusion.57 = (bf16[1,512,1536]{2,1,0:T(8,128)(2,1)S(1)}, bf16[1,512,1536]{2,1,0:T(8,128)(2,1)S(1)}) fusion(bf16[1,512,1536]{2,1,0:T(8,128)(2,1)S(1)} %bitcast.299, f32[1536]{0:T(1024)S(1)} %copy-done.7, f32[512]{0:T(512)S(1)} %rsqrt.41, f32[512]{0:T(512)S(1)} %rsqrt.44, bf16[1,512,1536]{2,1,0:T(8,128)(2,1)} %bitcast.37), kind=kLoop, calls=%fused_computation.75 | loop fusion | flops 18874368 | bytes 6301696 | tf_op jit(solution)/shard_map/convert_element_type | solution.py:57
  74.9 1.6 collective-permute-start.1
  76.5 4.8 %fusion.36 = (bf16[8,1,64,1536]{3,2,0,1:T(8,128)(2,1)}, bf16[8,1,64,1536]{3,2,0,1:T(8,128)(2,1)S(1)}) fusion(bf16[8,1,64,1536]{3,2,1,0:T(8,128)(2,1)S(1)} %all_to_all.30, f32[1536]{0:T(1024)S(1)} %copy-done.7, f32[8,64]{1,0:T(8,128)S(1)} %add_rsqrt_fusion.1, f32[8,64]{1,0:T(8,128)S(1)} %add_rsqrt_fusion, bf16[8,1,64,1536]{3,2,1,0:T(8,128)(2,1)} %all-to-all-done.3), kind=kLoop, calls=%fused_computation.54 | loop fusion | flops 18874368 | bytes 6301696 | tf_op jit(solution)/shard_map/convert_element_type | solution.py:57
  85.9 4.3 %all-to-all-start.4 = ((bf16[8,1,192,512]{3,2,1,0:T(8,128)(2,1)}), bf16[8,1,192,512]{3,2,1,0:T(8,128)(2,1)}, u32[]{:S(2)}, u32[]{:S(2)}) async-start(bf16[8,1,192,512]{3,2,1,0:T(8,128)(2,1)} %broadcast_in_dim.61), calls=%async_computation.4 | async-start | bytes 3145728 | tf_op jit(solution)/shard_map/all_to_all | solution.py:30
  90.3 2.2 fusion.166
  92.8 6.1 %collective-permute-start = (bf16[1,2,1536]{2,1,0:T(2,128)(2,1)S(1)}, bf16[1,2,1536]{2,1,0:T(2,128)(2,1)S(1)}, u32[]{:S(2)}, u32[]{:S(2)}) collective-permute-start(bf16[1,2,1536]{2,1,0:T(2,128)(2,1)S(1)} %get-tuple-element.343), channel_id=1, source_target_pairs={{0,8},{8,16},{16,24},{24,32},{32,40},{40,48},{48,56},{56,64},{64,7... | collective-permute-start | bytes 18440 | tf_op jit(solution)/shard_map/ppermute | solution.py:18
  98.9 2.2 fusion.97
  103.2 8.3 %all-to-all-done.4 = bf16[8,1,192,512]{3,2,1,0:T(8,128)(2,1)} async-done(((bf16[8,1,192,512]{3,2,1,0:T(8,128)(2,1)}), bf16[8,1,192,512]{3,2,1,0:T(8,128)(2,1)}, u32[]{:S(2)}, u32[]{:S(2)}) %all-to-all-start.4) | async-done | bytes 1572896 | tf_op jit(solution)/shard_map/all_to_all | solution.py:30
  111.5 1.3 broadcast_in_dim.29
  112.8 4.8 %all-to-all-start.1 = ((bf16[8,1,192,512]{3,2,1,0:T(8,128)(2,1)}), bf16[8,1,192,512]{3,2,1,0:T(8,128)(2,1)S(1)}, u32[]{:S(2)}, u32[]{:S(2)}) async-start(bf16[8,1,192,512]{3,2,1,0:T(8,128)(2,1)} %broadcast_in_dim.29), calls=%async_computation.1 | async-start | bytes 3145728 | tf_op jit(solution)/shard_map/all_to_all | solution.py:30
  117.8 1.8 multiply_reduce_fusion
  119.7 21.7 %all-to-all-done.1 = bf16[8,1,192,512]{3,2,1,0:T(8,128)(2,1)S(1)} async-done(((bf16[8,1,192,512]{3,2,1,0:T(8,128)(2,1)}), bf16[8,1,192,512]{3,2,1,0:T(8,128)(2,1)S(1)}, u32[]{:S(2)}, u32[]{:S(2)}) %all-to-all-start.1) | async-done | bytes 1572896 | tf_op jit(solution)/shard_map/all_to_all | solution.py:30
  142.5 1.8 bitcast_convert_fusion
  147.4 2.5 fusion.159
  151.3 1.5 fusion.149
  152.8 2.1 fusion.148
  154.9 2.2 fusion.157
  157.2 28.8 %all-gather.13.cloned.1.call-done = bf16[192,8192]{1,0:T(8,128)(2,1)} async-done(((bf16[192,512]{1,0:T(8,128)(2,1)}), bf16[192,8192]{1,0:T(8,128)(2,1)}) %all-gather.13.cloned.1.call-update) | async-done | bytes 3145744 | tf_op jit(solution)/shard_map/all_gather | solution.py:90
  186.0 37.6 %all-gather.15.cloned.1.call-done = bf16[192,8192]{1,0:T(8,128)(2,1)} async-done(((bf16[192,512]{1,0:T(8,128)(2,1)}), bf16[192,8192]{1,0:T(8,128)(2,1)}) %all-gather.15.cloned.1.call-update) | async-done | bytes 3145744 | tf_op jit(solution)/shard_map/all_gather | solution.py:91
  223.6 46.2 %while.37 = (s32[]{:T(128)}, f32[1,1,512]{2,1,0:T(1,128)S(1)}, f32[1,1,512]{2,1,0:T(1,128)S(1)}, f32[1,1,192,512]{3,2,1,0:T(8,128)S(1)}, bf16[1,192,8192]{2,1,0:...) while((s32[]{:T(128)}, f32[1,1,512]{2,1,0:T(1,128)S(1)}, ...), condition=%wide.region_12.0_spmd.clone, body=%wide.region_9.0_spmd.clone.sunk | while | flops 202934784 | bytes 4554935 | solution.py:119
  225.1 1.3 fusion.241
  228.0 1.3 fusion.241
  230.9 1.3 fusion.241
  233.8 1.4 fusion.241
  236.7 1.3 fusion.241
  239.6 1.3 fusion.241
  242.5 1.3 fusion.241
  245.4 1.3 fusion.241
  248.3 1.3 fusion.241
  251.1 1.3 fusion.241
  254.0 1.3 fusion.241
  256.9 1.3 fusion.241
  259.8 1.3 fusion.241
  262.7 1.3 fusion.241
  265.6 1.3 fusion.241
  268.4 1.3 fusion.241
  269.8 1.8 convolution_convert_fusion
  271.6 6.4 %all-to-all-start.5 = ((bf16[8,64,1,1536]{3,1,2,0:T(8,128)(2,1)}), bf16[8,64,1,1536]{3,1,2,0:T(8,128)(2,1)S(1)}, u32[]{:S(2)}, u32[]{:S(2)}) async-start(bf16[8,64,1,1536]{3,1,2,0:T(8,128)(2,1)} %bitcast.302), calls=%async_computation.5 | async-start | bytes 3145728 | tf_op jit(solution)/shard_map/all_to_all | solution.py:137
  278.0 25.9 %all-gather.11.cloned.1.call-done = bf16[192,8192]{1,0:T(8,128)(2,1)} async-done(((bf16[192,512]{1,0:T(8,128)(2,1)}), bf16[192,8192]{1,0:T(8,128)(2,1)}) %all-gather.11.cloned.1.call-update) | async-done | bytes 3145744 | tf_op jit(solution)/shard_map/all_gather | solution.py:91
  303.9 46.1 %while.36 = (s32[]{:T(128)}, f32[1,1,512]{2,1,0:T(1,128)S(1)}, f32[1,1,512]{2,1,0:T(1,128)S(1)}, f32[1,1,192,512]{3,2,1,0:T(8,128)S(1)}, bf16[1,192,8192]{2,1,0:...) while((s32[]{:T(128)}, f32[1,1,512]{2,1,0:T(1,128)S(1)}, ...), condition=%wide.region_5.0_spmd.clone, body=%wide.region_2.0_spmd.clone.sunk | while | flops 202934784 | bytes 4554935 | solution.py:119
  305.4 1.3 fusion.234
  308.3 1.3 fusion.234
  311.2 1.3 fusion.234
  314.0 1.3 fusion.234
  316.9 1.3 fusion.234
  319.8 1.3 fusion.234
  322.7 1.3 fusion.234
  325.6 1.3 fusion.234
  328.5 1.3 fusion.234
  331.4 1.3 fusion.234
  334.2 1.3 fusion.234
  337.1 1.3 fusion.234
  340.0 1.3 fusion.234
  342.9 1.3 fusion.234
  345.8 1.3 fusion.234
  348.7 1.3 fusion.234
  350.0 1.9 convolution_convert_fusion.1
  351.9 6.0 %all-to-all-start.2 = ((bf16[8,64,1,1536]{3,1,2,0:T(8,128)(2,1)}), bf16[8,64,1,1536]{3,1,2,0:T(8,128)(2,1)}, u32[]{:S(2)}, u32[]{:S(2)}) async-start(bf16[8,64,1,1536]{3,1,2,0:T(8,128)(2,1)} %bitcast.303), calls=%async_computation.2 | async-start | bytes 3145728 | tf_op jit(solution)/shard_map/all_to_all | solution.py:137
  360.8 20.4 %all-to-all-done.2 = bf16[8,64,1,1536]{3,1,2,0:T(8,128)(2,1)} async-done(((bf16[8,64,1,1536]{3,1,2,0:T(8,128)(2,1)}), bf16[8,64,1,1536]{3,1,2,0:T(8,128)(2,1)}, u32[]{:S(2)}, u32[]{:S(2)}) %all-to-all-start.2) | async-done | bytes 1572896 | tf_op jit(solution)/shard_map/all_to_all | solution.py:137
  381.3 1.7 convert_reduce_fusion.1
  (242 shorter events, 71.4 us)
Async XLA Ops:
  6.5 263.3 %copy-start = (bf16[192,1536]{1,0:T(8,128)(2,1)S(1)}, bf16[192,1536]{1,0:T(8,128)(2,1)}, u32[]{:S(2)}) copy-start(bf16[192,1536]{1,0:T(8,128)(2,1)} %param.19) | copy-start | bytes 1769476
  38.7 29.5 %copy-start.7 = (f32[1536]{0:T(1024)S(1)}, f32[1536]{0:T(1024)}, u32[]{:S(2)}) copy-start(f32[1536]{0:T(1024)} %param.13) | copy-start | bytes 18436
  38.7 26.4 %all-to-all-start.3 = ((bf16[8,1,64,1536]{3,2,1,0:T(8,128)(2,1)}), bf16[8,1,64,1536]{3,2,1,0:T(8,128)(2,1)}, u32[]{:S(2)}, u32[]{:S(2)}) async-start(bf16[8,1,64,1536]{3,2,1,0:T(8,128)(2,1)} %broadcast_in_dim.33), calls=%async_computation.3 | async-start | bytes 3145728 | tf_op jit(solution)/shard_map/all_to_all | solution.py:30
  72.2 9.0 %copy-start.5 = (bf16[1,512,1536]{2,1,0:T(8,128)(2,1)}, bf16[1,512,1536]{2,1,0:T(8,128)(2,1)S(1)}, u32[]{:S(2)}) copy-start(bf16[1,512,1536]{2,1,0:T(8,128)(2,1)S(1)} %get-tuple-element.353) | copy-start | bytes 4718596
  72.3 11.0 %collective-permute-start.2 = (bf16[1,2,1536]{2,1,0:T(2,128)(2,1)S(1)}, bf16[1,2,1536]{2,1,0:T(2,128)(2,1)S(1)}, u32[]{:S(2)}, u32[]{:S(2)}) collective-permute-start(bf16[1,2,1536]{2,1,0:T(2,128)(2,1)S(1)} %get-tuple-element.345), channel_id=1, source_target_pairs={{0,8},{8,16},{16,24},{24,32},{32,40},{40,48},{48,56},{56,64},{64,7... | collective-permute-start | bytes 18440 | tf_op jit(solution)/shard_map/ppermute | solution.py:18
  73.6 8.3 %collective-permute-start.3 = (bf16[1,2,1536]{2,1,0:T(2,128)(2,1)S(1)}, bf16[1,2,1536]{2,1,0:T(2,128)(2,1)S(1)}, u32[]{:S(2)}, u32[]{:S(2)}) collective-permute-start(bf16[1,2,1536]{2,1,0:T(2,128)(2,1)S(1)} %get-tuple-element.346), channel_id=1, source_target_pairs={{8,0},{16,8},{24,16},{32,24},{40,32},{48,40},{56,48},{64,56},{72,6... | collective-permute-start | bytes 18440 | tf_op jit(solution)/shard_map/ppermute | solution.py:20
  74.9 6.4 %copy-start.9 = (bf16[5,192,1536]{2,1,0:T(8,128)(2,1)S(1)}, bf16[5,192,1536]{2,1,0:T(8,128)(2,1)}, u32[]{:S(2)}) copy-start(bf16[5,192,1536]{2,1,0:T(8,128)(2,1)} %param.14) | copy-start | bytes 8847364
  74.9 24.0 %collective-permute-start.1 = (bf16[1,2,1536]{2,1,0:T(2,128)(2,1)S(1)}, bf16[1,2,1536]{2,1,0:T(2,128)(2,1)S(1)}, u32[]{:S(2)}, u32[]{:S(2)}) collective-permute-start(bf16[1,2,1536]{2,1,0:T(2,128)(2,1)S(1)} %get-tuple-element.344), channel_id=1, source_target_pairs={{8,0},{16,8},{24,16},{32,24},{40,32},{48,40},{56,48},{64,56},{72,6... | collective-permute-start | bytes 18440 | tf_op jit(solution)/shard_map/ppermute | solution.py:20
  85.9 25.6 %all-to-all-start.4 = ((bf16[8,1,192,512]{3,2,1,0:T(8,128)(2,1)}), bf16[8,1,192,512]{3,2,1,0:T(8,128)(2,1)}, u32[]{:S(2)}, u32[]{:S(2)}) async-start(bf16[8,1,192,512]{3,2,1,0:T(8,128)(2,1)} %broadcast_in_dim.61), calls=%async_computation.4 | async-start | bytes 3145728 | tf_op jit(solution)/shard_map/all_to_all | solution.py:30
  92.6 8.5 %copy-start.6 = (bf16[1,512,1536]{2,1,0:T(8,128)(2,1)S(1)}, bf16[1,512,1536]{2,1,0:T(8,128)(2,1)}, u32[]{:S(2)}) copy-start(bf16[1,512,1536]{2,1,0:T(8,128)(2,1)} %copy-done.5) | copy-start | bytes 4718596
  92.8 8.4 %copy-start.10 = (bf16[5,192,1536]{2,1,0:T(8,128)(2,1)S(1)}, bf16[5,192,1536]{2,1,0:T(8,128)(2,1)}, u32[]{:S(2)}) copy-start(bf16[5,192,1536]{2,1,0:T(8,128)(2,1)} %param.14) | copy-start | bytes 8847364
  92.8 8.3 %collective-permute-start = (bf16[1,2,1536]{2,1,0:T(2,128)(2,1)S(1)}, bf16[1,2,1536]{2,1,0:T(2,128)(2,1)S(1)}, u32[]{:S(2)}, u32[]{:S(2)}) collective-permute-start(bf16[1,2,1536]{2,1,0:T(2,128)(2,1)S(1)} %get-tuple-element.343), channel_id=1, source_target_pairs={{0,8},{8,16},{16,24},{24,32},{32,40},{40,48},{48,56},{56,64},{64,7... | collective-permute-start | bytes 18440 | tf_op jit(solution)/shard_map/ppermute | solution.py:18
  112.8 28.6 %all-to-all-start.1 = ((bf16[8,1,192,512]{3,2,1,0:T(8,128)(2,1)}), bf16[8,1,192,512]{3,2,1,0:T(8,128)(2,1)S(1)}, u32[]{:S(2)}, u32[]{:S(2)}) async-start(bf16[8,1,192,512]{3,2,1,0:T(8,128)(2,1)} %broadcast_in_dim.29), calls=%async_computation.1 | async-start | bytes 3145728 | tf_op jit(solution)/shard_map/all_to_all | solution.py:30
  117.6 68.4 %all-gather.13.cloned.1.call-start = ((), (), s32[]{:S(2)}) async-start(), calls=%async_computation.8 | async-start | bytes 3342336 | tf_op jit(solution)/shard_map/all_gather | solution.py:90
  141.4 1.2 copy-start.2
  142.5 1.9 copy-start.8
  144.4 1.8 copy-start.3
  144.4 3.0 copy-start.4
  145.0 1.2 copy-start.1
  147.3 76.3 %all-gather.15.cloned.1.call-start = ((), (), s32[]{:S(2)}) async-start(), calls=%async_computation.9 | async-start | bytes 3342336 | tf_op jit(solution)/shard_map/all_gather | solution.py:91
  150.0 128.0 %all-gather.9.cloned.1.call-start = ((), (), s32[]{:S(2)}) async-start(), calls=%async_computation.6 | async-start | bytes 3342336 | tf_op jit(solution)/shard_map/all_gather | solution.py:90
  151.2 152.7 %all-gather.11.cloned.1.call-start = ((), (), s32[]{:S(2)}) async-start(), calls=%async_computation.7 | async-start | bytes 3342336 | tf_op jit(solution)/shard_map/all_gather | solution.py:91
  271.6 80.3 %all-to-all-start.5 = ((bf16[8,64,1,1536]{3,1,2,0:T(8,128)(2,1)}), bf16[8,64,1,1536]{3,1,2,0:T(8,128)(2,1)S(1)}, u32[]{:S(2)}, u32[]{:S(2)}) async-start(bf16[8,64,1,1536]{3,1,2,0:T(8,128)(2,1)} %bitcast.302), calls=%async_computation.5 | async-start | bytes 3145728 | tf_op jit(solution)/shard_map/all_to_all | solution.py:137
  351.9 29.4 %all-to-all-start.2 = ((bf16[8,64,1,1536]{3,1,2,0:T(8,128)(2,1)}), bf16[8,64,1,1536]{3,1,2,0:T(8,128)(2,1)}, u32[]{:S(2)}, u32[]{:S(2)}) async-start(bf16[8,64,1,1536]{3,1,2,0:T(8,128)(2,1)} %bitcast.303), calls=%async_computation.2 | async-start | bytes 3145728 | tf_op jit(solution)/shard_map/all_to_all | solution.py:137
Sparse Core Ops, SparseCore 0:
  147.5 38.4 all-gather.12
  187.7 35.9 all-gather.14
  225.3 35.9 all-gather.8
  262.8 41.0 all-gather.10
where the time goes:
time: 393 us; the launch traced here: 390 us
  waiting for transfers between devices  164 us (42%)
  matrix products  108 us (27%)
  starting transfers between devices  36.5 us (9%)
  blocking collectives  29.6 us (8%)
  other arithmetic  25.9 us (7%)
  between operations  13.6 us (3%)
  local copies, waits for them, and re-layouts  11.1 us (3%)
    all_gather x2, waiting for transfers between devices, one_sample(): value_tile = lax.all_gather(value_rows, 'seq', axis=2, tiled=True)  63.6 us
    all_to_all x3, waiting for transfers between devices, gather_batch(): lax.all_to_all(copies, 'batch', 0, 0, tiled=False)  51.4 us
    dot_general x32, matrix products, consume(): jnp.einsum('shqk,shdk->shdq', weights.astype(jnp.bfloat16), value_block,...  42.8 us
    dot_general x32, matrix products, consume(): jnp.einsum('shdq,shdk->shqk', query_heads, key_block, preferred_element_t...  40.8 us
    all_to_all x1, blocking collectives, gather_batch(): lax.all_to_all(copies, 'batch', 0, 0, tiled=False)  29.6 us
    all_gather x2, waiting for transfers between devices, one_sample(): key_tile = lax.all_gather(key_rows, 'seq', axis=2, tiled=True)  28.8 us
    all_to_all x2, waiting for transfers between devices, one_sample(): lax.all_to_all(partial_rows, 'batch', 0, 0, tiled=False).astype(jnp.float32)  20.4 us
    all_to_all x3, starting transfers between devices, gather_batch(): lax.all_to_all(copies, 'batch', 0, 0, tiled=False)  13.5 us
  transfers between devices with their start and end apart: 13, of which 7 were waited for; matrix products, arithmetic and copies ran while one was open for 32% of the time, Pallas kernels for 0%

commit v1 on v0

--- a/solution.py
+++ b/solution.py
@@ -87,7 +87,9 @@
     start_max = jnp.full((sample_count, heads_here, seq_rows), -jnp.inf, jnp.float32)
     start_sum = jnp.zeros((sample_count, heads_here, seq_rows), jnp.float32)
     start_acc = jnp.zeros((sample_count, heads_here, HD, seq_rows), jnp.float32)
-    key_tile = lax.all_gather(key_rows, "seq", axis=2, tiled=True)
+    upper = jnp.stack([key_rows for _ in range(lax.psum(1, "seq"))], axis=0)
+    inter = lax.all_to_all(upper, "seq", 0, 0)
+    key_tile = jnp.concatenate(inter, 2)
     value_tile = lax.all_gather(value_rows, "seq", axis=2, tiled=True)
     key_count = key_tile.shape[2]
     block_rows = math.gcd(key_count, 512)

time: 393 us -> 425 us (1.081)
  local copies, waits for them, and re-layouts: 11.1 us -> 23.9 us
  waiting for transfers between devices: 164 us -> 175 us
  starting transfers between devices: 36.5 us -> 42.3 us
    all_to_all x0 -> x2, waiting for transfers between devices: none -> 98.2 us  [one_sample(): inter = lax.all_to_all(upper, 'seq', 0, 0)]
    all_gather x2, waiting for transfers between devices: 63.6 us -> 0.02 us  [one_sample(): value_tile = lax.all_gather(value_rows, 'seq', axis=2, tiled=True)]
    all_gather x2 -> x0, waiting for transfers between devices: 28.8 us -> none  [one_sample(): key_tile = lax.all_gather(key_rows, 'seq', axis=2, tiled=True)]
    all_to_all x0 -> x2, starting transfers between devices: none -> 9.37 us  [one_sample(): inter = lax.all_to_all(upper, 'seq', 0, 0)]
    reshape x0 -> x2, local copies, waits for them, and re-layouts: none -> 7.98 us  [one_sample(): key_tile = jnp.concatenate(inter, 2)]
    all_to_all x3, waiting for transfers between devices: 51.4 us -> 59.4 us  [gather_batch(): lax.all_to_all(copies, 'batch', 0, 0, tiled=False)]
  transfers between devices with their start and end apart: 13 -> 13, of which waited for: 7 -> 6; matrix products, arithmetic and copies ran while one was open for 32% -> 34% of each run, Pallas kernels for 0% -> 0%
where the time goes in v1:
time: 425 us; the launch traced here: 421 us
  waiting for transfers between devices  175 us (41%)
  matrix products  109 us (26%)
  starting transfers between devices  42.3 us (10%)
  blocking collectives  29.6 us (7%)
  other arithmetic  26 us (6%)
  local copies, waits for them, and re-layouts  23.9 us (6%)
  between operations  13.9 us (3%)
    all_to_all x2, waiting for transfers between devices, one_sample(): inter = lax.all_to_all(upper, 'seq', 0, 0)  98.2 us
    all_to_all x3, waiting for transfers between devices, gather_batch(): lax.all_to_all(copies, 'batch', 0, 0, tiled=False)  59.4 us
    dot_general x32, matrix products, consume(): jnp.einsum('shqk,shdk->shdq', weights.astype(jnp.bfloat16), value_block,...  42.7 us
    dot_general x32, matrix products, consume(): jnp.einsum('shdq,shdk->shqk', query_heads, key_block, preferred_element_t...  40.7 us
    all_to_all x1, blocking collectives, gather_batch(): lax.all_to_all(copies, 'batch', 0, 0, tiled=False)  29.6 us
    all_to_all x2, waiting for transfers between devices, one_sample(): lax.all_to_all(partial_rows, 'batch', 0, 0, tiled=False).astype(jnp.float32)  16.9 us
    dot_general x10, matrix products, one_sample(): jnp.einsum('std,ed->set', framed[:, offset:offset + seq_rows], conv_weigh...  12.8 us
    all_to_all x3, starting transfers between devices, gather_batch(): lax.all_to_all(copies, 'batch', 0, 0, tiled=False)  12.3 us
  transfers between devices with their start and end apart: 13, of which 6 were waited for; matrix products, arithmetic and copies ran while one was open for 34% of the time, Pallas kernels for 0%

profile of v1, /device:TPU:0, one launch (start us, length us, event | category | flops | bytes accessed | tf_op | source)
XLA Modules:
  0.0 421.2 jit_solution(14503390122080786499)
XLA Ops:
  7.8 29.6 %all_to_all.40 = bf16[8,1,64,1536]{3,2,1,0:T(8,128)(2,1)S(1)} all-to-all(bf16[8,1,64,1536]{3,2,1,0:T(8,128)(2,1)S(1)} %broadcast_in_dim.27), channel_id=1, replica_groups=mesh['seq'=16,'batch'=8] {'batch'}, dimensions={0} | all-to-all | bytes 3145728 | tf_op jit(solution)/shard_map/all_to_all | solution.py:30
  38.7 4.4 %all-to-all-start.4 = ((bf16[8,1,64,1536]{3,2,1,0:T(8,128)(2,1)}), bf16[8,1,64,1536]{3,2,1,0:T(8,128)(2,1)}, u32[]{:S(2)}, u32[]{:S(2)}) async-start(bf16[8,1,64,1536]{3,2,1,0:T(8,128)(2,1)} %broadcast_in_dim.33), calls=%async_computation.4 | async-start | bytes 3145728 | tf_op jit(solution)/shard_map/all_to_all | solution.py:30
  43.6 21.5 %all-to-all-done.4 = bf16[8,1,64,1536]{3,2,1,0:T(8,128)(2,1)} async-done(((bf16[8,1,64,1536]{3,2,1,0:T(8,128)(2,1)}), bf16[8,1,64,1536]{3,2,1,0:T(8,128)(2,1)}, u32[]{:S(2)}, u32[]{:S(2)}) %all-to-all-start.4) | async-done | bytes 1572896 | tf_op jit(solution)/shard_map/all_to_all | solution.py:30
  65.1 1.8 fusion.41
  67.0 4.0 fusion.57
  72.3 3.0 collective-permute-start.2
  75.4 3.4 collective-permute-start
  80.1 4.8 %fusion.36 = (bf16[8,1,64,1536]{3,2,0,1:T(8,128)(2,1)}, bf16[8,1,64,1536]{3,2,0,1:T(8,128)(2,1)S(1)}) fusion(bf16[8,1,64,1536]{3,2,1,0:T(8,128)(2,1)S(1)} %all_to_all.40, f32[1536]{0:T(1024)S(1)} %copy-done.9, f32[8,64]{1,0:T(8,128)S(1)} %add_rsqrt_fusion.1, f32[8,64]{1,0:T(8,128)S(1)} %add_rsqrt_fusion, bf16[8,1,64,1536]{3,2,1,0:T(8,128)(2,1)} %all-to-all-done.4), kind=kLoop, calls=%fused_computation.54 | loop fusion | flops 18874368 | bytes 6301696 | tf_op jit(solution)/shard_map/convert_element_type | solution.py:57
  84.9 1.7 fusion.164
  87.9 2.4 fusion.74
  94.2 4.3 %all-to-all-start.5 = ((bf16[8,1,192,512]{3,2,1,0:T(8,128)(2,1)}), bf16[8,1,192,512]{3,2,1,0:T(8,128)(2,1)}, u32[]{:S(2)}, u32[]{:S(2)}) async-start(bf16[8,1,192,512]{3,2,1,0:T(8,128)(2,1)} %broadcast_in_dim.61), calls=%async_computation.5 | async-start | bytes 3145728 | tf_op jit(solution)/shard_map/all_to_all | solution.py:30
  98.5 2.2 fusion.166
  101.1 2.3 fusion.101
  106.0 16.6 %all-to-all-done.5 = bf16[8,1,192,512]{3,2,1,0:T(8,128)(2,1)} async-done(((bf16[8,1,192,512]{3,2,1,0:T(8,128)(2,1)}), bf16[8,1,192,512]{3,2,1,0:T(8,128)(2,1)}, u32[]{:S(2)}, u32[]{:S(2)}) %all-to-all-start.5) | async-done | bytes 1572896 | tf_op jit(solution)/shard_map/all_to_all | solution.py:30
  124.0 3.6 all-to-all-start.1
  127.8 1.8 multiply_reduce_fusion
  129.6 21.3 %all-to-all-done.1 = bf16[8,1,192,512]{3,2,1,0:T(8,128)(2,1)S(1)} async-done(((bf16[8,1,192,512]{3,2,1,0:T(8,128)(2,1)}), bf16[8,1,192,512]{3,2,1,0:T(8,128)(2,1)S(1)}, u32[]{:S(2)}, u32[]{:S(2)}) %all-to-all-start.1) | async-done | bytes 1572896 | tf_op jit(solution)/shard_map/all_to_all | solution.py:30
  151.3 2.0 bitcast_convert_fusion
  156.9 1.9 fusion.156
  158.8 1.9 stack.4
  160.7 4.9 %all-to-all-start.2 = ((bf16[16,1,192,512]{3,2,1,0:T(8,128)(2,1)}), bf16[16,1,192,512]{3,2,1,0:T(8,128)(2,1)}, u32[]{:S(2)}, u32[]{:S(2)}) async-start(bf16[16,1,192,512]{3,2,1,0:T(8,128)(2,1)} %stack.4), calls=%async_computation.2 | async-start | bytes 6291456 | tf_op jit(solution)/shard_map/all_to_all | solution.py:91
  166.1 55.9 %all-to-all-done.2 = bf16[16,1,192,512]{3,2,1,0:T(8,128)(2,1)} async-done(((bf16[16,1,192,512]{3,2,1,0:T(8,128)(2,1)}), bf16[16,1,192,512]{3,2,1,0:T(8,128)(2,1)}, u32[]{:S(2)}, u32[]{:S(2)}) %all-to-all-start.2) | async-done | bytes 3145760 | tf_op jit(solution)/shard_map/all_to_all | solution.py:91
  222.0 2.0 stack.5
  224.0 4.5 %all-to-all-start.6 = ((bf16[16,1,192,512]{3,2,1,0:T(8,128)(2,1)}), bf16[16,1,192,512]{3,2,1,0:T(8,128)(2,1)}, u32[]{:S(2)}, u32[]{:S(2)}) async-start(bf16[16,1,192,512]{3,2,1,0:T(8,128)(2,1)} %stack.5), calls=%async_computation.6 | async-start | bytes 6291456 | tf_op jit(solution)/shard_map/all_to_all | solution.py:91
  228.6 2.2 fusion.159
  230.9 2.1 fusion.149
  232.9 1.5 fusion.148
  234.5 3.9 copy.46
  238.4 42.2 %all-to-all-done.6 = bf16[16,1,192,512]{3,2,1,0:T(8,128)(2,1)} async-done(((bf16[16,1,192,512]{3,2,1,0:T(8,128)(2,1)}), bf16[16,1,192,512]{3,2,1,0:T(8,128)(2,1)}, u32[]{:S(2)}, u32[]{:S(2)}) %all-to-all-start.6) | async-done | bytes 3145760 | tf_op jit(solution)/shard_map/all_to_all | solution.py:91
  280.7 4.0 copy.47
  284.7 46.1 %while.36 = (s32[]{:T(128)}, f32[1,1,512]{2,1,0:T(1,128)S(1)}, f32[1,1,512]{2,1,0:T(1,128)S(1)}, f32[1,1,192,512]{3,2,1,0:T(8,128)S(1)}, bf16[1,192,8192]{2,1,0:...) while((s32[]{:T(128)}, f32[1,1,512]{2,1,0:T(1,128)S(1)}, ...), condition=%wide.region_5.0_spmd.clone, body=%wide.region_2.0_spmd.clone.sunk | while | flops 202934784 | bytes 4554927 | solution.py:121
  286.2 1.3 fusion.234
  289.1 1.3 fusion.234
  294.9 1.3 fusion.234
  297.8 1.3 fusion.234
  300.6 1.3 fusion.234
  303.5 1.3 fusion.234
  306.4 1.3 fusion.234
  309.3 1.3 fusion.234
  315.1 1.3 fusion.234
  317.9 1.3 fusion.234
  320.8 1.3 fusion.234
  323.7 1.3 fusion.234
  329.5 1.3 fusion.234
  330.9 1.9 convolution_convert_fusion.1
  332.7 4.3 %all-to-all-start.3 = ((bf16[8,64,1,1536]{3,1,2,0:T(8,128)(2,1)}), bf16[8,64,1,1536]{3,1,2,0:T(8,128)(2,1)}, u32[]{:S(2)}, u32[]{:S(2)}) async-start(bf16[8,64,1,1536]{3,1,2,0:T(8,128)(2,1)} %bitcast.33), calls=%async_computation.3 | async-start | bytes 3145728 | tf_op jit(solution)/shard_map/all_to_all | solution.py:139
  337.0 46.2 %while.37 = (s32[]{:T(128)}, f32[1,1,512]{2,1,0:T(1,128)S(1)}, f32[1,1,512]{2,1,0:T(1,128)S(1)}, f32[1,1,192,512]{3,2,1,0:T(8,128)S(1)}, bf16[1,192,8192]{2,1,0:...) while((s32[]{:T(128)}, f32[1,1,512]{2,1,0:T(1,128)S(1)}, ...), condition=%wide.region_12.0_spmd.clone, body=%wide.region_9.0_spmd.clone.sunk | while | flops 202934784 | bytes 4554927 | solution.py:121
  338.6 1.3 fusion.241
  341.5 1.3 fusion.241
  347.2 1.3 fusion.241
  350.1 1.3 fusion.241
  353.0 1.3 fusion.241
  355.9 1.3 fusion.241
  361.7 1.3 fusion.241
  364.5 1.3 fusion.241
  367.4 1.3 fusion.241
  370.3 1.3 fusion.241
  376.1 1.3 fusion.241
  379.0 1.3 fusion.241
  381.9 1.3 fusion.241
  383.2 1.8 convolution_convert_fusion
  385.0 7.0 %all-to-all-start.7 = ((bf16[8,64,1,1536]{3,1,2,0:T(8,128)(2,1)}), bf16[8,64,1,1536]{3,1,2,0:T(8,128)(2,1)S(1)}, u32[]{:S(2)}, u32[]{:S(2)}) async-start(bf16[8,64,1,1536]{3,1,2,0:T(8,128)(2,1)} %bitcast.308), calls=%async_computation.7 | async-start | bytes 3145728 | tf_op jit(solution)/shard_map/all_to_all | solution.py:139
  394.7 1.7 convert_reduce_fusion.1
  396.5 16.9 %all-to-all-done.7 = bf16[8,64,1,1536]{3,1,2,0:T(8,128)(2,1)S(1)} async-done(((bf16[8,64,1,1536]{3,1,2,0:T(8,128)(2,1)}), bf16[8,64,1,1536]{3,1,2,0:T(8,128)(2,1)S(1)}, u32[]{:S(2)}, u32[]{:S(2)}) %all-to-all-start.7) | async-done | bytes 1572896 | tf_op jit(solution)/shard_map/all_to_all | solution.py:139
  (248 shorter events, 79.5 us)
Async XLA Ops:
  6.5 324.3 %copy-start = (bf16[192,1536]{1,0:T(8,128)(2,1)S(1)}, bf16[192,1536]{1,0:T(8,128)(2,1)}, u32[]{:S(2)}) copy-start(bf16[192,1536]{1,0:T(8,128)(2,1)} %param.19) | copy-start | bytes 1769476
  38.7 28.2 %copy-start.9 = (f32[1536]{0:T(1024)S(1)}, f32[1536]{0:T(1024)}, u32[]{:S(2)}) copy-start(f32[1536]{0:T(1024)} %param.13) | copy-start | bytes 18436
  38.7 26.4 %all-to-all-start.4 = ((bf16[8,1,64,1536]{3,2,1,0:T(8,128)(2,1)}), bf16[8,1,64,1536]{3,2,1,0:T(8,128)(2,1)}, u32[]{:S(2)}, u32[]{:S(2)}) async-start(bf16[8,1,64,1536]{3,2,1,0:T(8,128)(2,1)} %broadcast_in_dim.33), calls=%async_computation.4 | async-start | bytes 3145728 | tf_op jit(solution)/shard_map/all_to_all | solution.py:30
  71.0 13.9 %copy-start.5 = (bf16[1,512,1536]{2,1,0:T(8,128)(2,1)}, bf16[1,512,1536]{2,1,0:T(8,128)(2,1)S(1)}, u32[]{:S(2)}) copy-start(bf16[1,512,1536]{2,1,0:T(8,128)(2,1)S(1)} %get-tuple-element.353) | copy-start | bytes 4718596
  71.0 13.9 %copy-start.7 = (bf16[1,512,1536]{2,1,0:T(8,128)(2,1)}, bf16[1,512,1536]{2,1,0:T(8,128)(2,1)S(1)}, u32[]{:S(2)}) copy-start(bf16[1,512,1536]{2,1,0:T(8,128)(2,1)S(1)} %get-tuple-element.354) | copy-start | bytes 4718596
  71.0 16.9 %collective-permute-start.3 = (bf16[1,2,1536]{2,1,0:T(2,128)(2,1)S(1)}, bf16[1,2,1536]{2,1,0:T(2,128)(2,1)S(1)}, u32[]{:S(2)}, u32[]{:S(2)}) collective-permute-start(bf16[1,2,1536]{2,1,0:T(2,128)(2,1)S(1)} %get-tuple-element.346), channel_id=1, source_target_pairs={{8,0},{16,8},{24,16},{32,24},{40,32},{48,40},{56,48},{64,56},{72,6... | collective-permute-start | bytes 18440 | tf_op jit(solution)/shard_map/ppermute | solution.py:20
  72.3 19.2 %collective-permute-start.2 = (bf16[1,2,1536]{2,1,0:T(2,128)(2,1)S(1)}, bf16[1,2,1536]{2,1,0:T(2,128)(2,1)S(1)}, u32[]{:S(2)}, u32[]{:S(2)}) collective-permute-start(bf16[1,2,1536]{2,1,0:T(2,128)(2,1)S(1)} %get-tuple-element.345), channel_id=1, source_target_pairs={{0,8},{8,16},{16,24},{24,32},{32,40},{40,48},{48,56},{56,64},{64,7... | collective-permute-start | bytes 18440 | tf_op jit(solution)/shard_map/ppermute | solution.py:18
  75.4 25.7 %collective-permute-start = (bf16[1,2,1536]{2,1,0:T(2,128)(2,1)S(1)}, bf16[1,2,1536]{2,1,0:T(2,128)(2,1)S(1)}, u32[]{:S(2)}, u32[]{:S(2)}) collective-permute-start(bf16[1,2,1536]{2,1,0:T(2,128)(2,1)S(1)} %get-tuple-element.343), channel_id=1, source_target_pairs={{0,8},{8,16},{16,24},{24,32},{32,40},{40,48},{48,56},{56,64},{64,7... | collective-permute-start | bytes 18440 | tf_op jit(solution)/shard_map/ppermute | solution.py:18
  78.8 24.6 %collective-permute-start.1 = (bf16[1,2,1536]{2,1,0:T(2,128)(2,1)S(1)}, bf16[1,2,1536]{2,1,0:T(2,128)(2,1)S(1)}, u32[]{:S(2)}, u32[]{:S(2)}) collective-permute-start(bf16[1,2,1536]{2,1,0:T(2,128)(2,1)S(1)} %get-tuple-element.344), channel_id=1, source_target_pairs={{8,0},{16,8},{24,16},{32,24},{40,32},{48,40},{56,48},{64,56},{72,6... | collective-permute-start | bytes 18440 | tf_op jit(solution)/shard_map/ppermute | solution.py:20
  87.9 2.4 copy-start.8
  87.9 3.0 copy-start.11
  94.2 28.4 %all-to-all-start.5 = ((bf16[8,1,192,512]{3,2,1,0:T(8,128)(2,1)}), bf16[8,1,192,512]{3,2,1,0:T(8,128)(2,1)}, u32[]{:S(2)}, u32[]{:S(2)}) async-start(bf16[8,1,192,512]{3,2,1,0:T(8,128)(2,1)} %broadcast_in_dim.61), calls=%async_computation.5 | async-start | bytes 3145728 | tf_op jit(solution)/shard_map/all_to_all | solution.py:30
  100.9 2.5 copy-start.6
  101.0 2.9 copy-start.12
  124.0 26.9 %all-to-all-start.1 = ((bf16[8,1,192,512]{3,2,1,0:T(8,128)(2,1)}), bf16[8,1,192,512]{3,2,1,0:T(8,128)(2,1)S(1)}, u32[]{:S(2)}, u32[]{:S(2)}) async-start(bf16[8,1,192,512]{3,2,1,0:T(8,128)(2,1)} %broadcast_in_dim.29), calls=%async_computation.1 | async-start | bytes 3145728 | tf_op jit(solution)/shard_map/all_to_all | solution.py:30
  127.6 157.1 %all-gather.5.cloned.1.call-start = ((), (), s32[]{:S(2)}) async-start(), calls=%async_computation.8 | async-start | bytes 3342336 | tf_op jit(solution)/shard_map/all_gather | solution.py:93
  150.9 2.4 copy-start.2
  153.3 0.7 copy-start.10
  154.0 1.7 copy-start.4
  154.0 2.9 copy-start.3
  154.6 1.1 copy-start.1
  160.7 61.3 %all-to-all-start.2 = ((bf16[16,1,192,512]{3,2,1,0:T(8,128)(2,1)}), bf16[16,1,192,512]{3,2,1,0:T(8,128)(2,1)}, u32[]{:S(2)}, u32[]{:S(2)}) async-start(bf16[16,1,192,512]{3,2,1,0:T(8,128)(2,1)} %stack.4), calls=%async_computation.2 | async-start | bytes 6291456 | tf_op jit(solution)/shard_map/all_to_all | solution.py:91
  224.0 56.7 %all-to-all-start.6 = ((bf16[16,1,192,512]{3,2,1,0:T(8,128)(2,1)}), bf16[16,1,192,512]{3,2,1,0:T(8,128)(2,1)}, u32[]{:S(2)}, u32[]{:S(2)}) async-start(bf16[16,1,192,512]{3,2,1,0:T(8,128)(2,1)} %stack.5), calls=%async_computation.6 | async-start | bytes 6291456 | tf_op jit(solution)/shard_map/all_to_all | solution.py:91
  228.5 108.5 %all-gather.7.cloned.1.call-start = ((), (), s32[]{:S(2)}) async-start(), calls=%async_computation.9 | async-start | bytes 3342336 | tf_op jit(solution)/shard_map/all_gather | solution.py:93
  332.7 52.3 %all-to-all-start.3 = ((bf16[8,64,1,1536]{3,1,2,0:T(8,128)(2,1)}), bf16[8,64,1,1536]{3,1,2,0:T(8,128)(2,1)}, u32[]{:S(2)}, u32[]{:S(2)}) async-start(bf16[8,64,1,1536]{3,1,2,0:T(8,128)(2,1)} %bitcast.33), calls=%async_computation.3 | async-start | bytes 3145728 | tf_op jit(solution)/shard_map/all_to_all | solution.py:139
  385.0 28.3 %all-to-all-start.7 = ((bf16[8,64,1,1536]{3,1,2,0:T(8,128)(2,1)}), bf16[8,64,1,1536]{3,1,2,0:T(8,128)(2,1)S(1)}, u32[]{:S(2)}, u32[]{:S(2)}) async-start(bf16[8,64,1,1536]{3,1,2,0:T(8,128)(2,1)} %bitcast.308), calls=%async_computation.7 | async-start | bytes 3145728 | tf_op jit(solution)/shard_map/all_to_all | solution.py:139
Sparse Core Ops, SparseCore 0:
  157.0 64.2 all-gather.4
  231.0 56.9 all-gather.6
